TPU v7x, 128 devices: a whole 4x4x4 slice. The times are simulated.
128 devices in a mesh: dp: 32 (over y, x, core), mp: 4 (over z).
Axes of the slice: x: 4, y: 4, z: 4, core: 2. Of those that a mesh axis runs over, the one named last changes fastest.
Arguments:
- hidden: bfloat16 [4096, 2560], P('dp', 'mp'), may hold values from -6 to 6
- norm_gain: bfloat16 [2560], replicated, may hold values from 0.5 to 1.5
- shared_gate: bfloat16 [2560, 3072], P(None, 'mp'), may hold values from -0.125 to 0.125
- shared_up: bfloat16 [2560, 3072], P(None, 'mp'), may hold values from -0.125 to 0.125
- shared_down: bfloat16 [3072, 2560], P('mp'), may hold values from -0.109375 to 0.109375
- expert_gate: bfloat16 [64, 2560, 1536], P('dp', None, 'mp'), may hold values from -0.125 to 0.125
- expert_up: bfloat16 [64, 2560, 1536], P('dp', None, 'mp'), may hold values from -0.125 to 0.125
- expert_down: bfloat16 [64, 1536, 2560], P('dp', 'mp'), may hold values from -0.15625 to 0.15625
- adapter_in: bfloat16 [64, 3072, 16], P('dp', 'mp'), may hold values from -0.109375 to 0.109375
- adapter_out: bfloat16 [64, 16, 2560], P('dp'), may hold values from -1.5 to 1.5
- active: int32 [16], replicated, may hold values from 0 to 63, as said below
- lengths: int32 [64], replicated, may hold values from 1 to 1024, 4096 in all
- request_adapter: int32 [64], replicated, may hold values from 0 to 15
- routes: int32 [4096, 6], P('dp'), may hold values from 0 to 63, all different within a row; in each aligned block of 128 rows (0 to 127, 128 to 255, ...) at most 16 rows name the same one
- route_weights: float32 [4096, 6], P('dp'), may hold values from 0.05 to 0.35
Outputs:
- layer_out: bfloat16 [4096, 2560], P('dp', 'mp')
Inputs may be any that keep to these rules, and one draw needn't show every extreme that they name: `active`: the entries are distinct. `routes`: within the 128 rows of one index of dp no expert is named more than 16 times, and that many is reached; a row names distinct experts.
All inputs are finite; a program needn't handle non-finite values.
Results may differ from a plain program's by a relative error of at most 0.015.
Values may be sent and summed in bfloat16 or wider, within the bound.
No kernel may reach another device: no remote copies, remote signals or barrier semaphores. Data moves between devices by JAX's collectives and lax.ppermute only.
A program may use at most 128 MiB of HBM per device.

v0:
```python
import jax
import jax.numpy as jnp
from jax import lax
from jax.sharding import PartitionSpec as P


def experts_apply(slots_in, expert_gate, expert_up, expert_down):
    gate_val = jnp.einsum(
        "sjcd,jdf->sjcf", slots_in, expert_gate, preferred_element_type=jnp.float32
    )
    up_val = jnp.einsum("sjcd,jdf->sjcf", slots_in, expert_up, preferred_element_type=jnp.float32)
    inner = (jax.nn.silu(gate_val) * up_val).astype(jnp.bfloat16)
    return jnp.einsum("sjcf,jfd->sjcd", inner, expert_down, preferred_element_type=jnp.float32)


def body(
    hidden,
    norm_gain,
    shared_gate,
    shared_up,
    shared_down,
    expert_gate,
    expert_up,
    expert_down,
    adapter_in,
    adapter_out,
    active,
    lengths,
    request_adapter,
    routes,
    route_weights,
):
    tok_rows = routes.shape[0]
    top_count = routes.shape[1]
    dp_count = lax.axis_size("dp")
    mp_count = lax.axis_size("mp")
    dp_index = lax.axis_index("dp")
    mp_index = lax.axis_index("mp")
    local_experts = expert_gate.shape[0]
    total_experts = local_experts * dp_count
    capacity = mp_count * max(1, tok_rows * top_count * 4 // (total_experts * mp_count * 3))
    col_width = hidden.shape[1]
    col_start = mp_index * col_width
    active_count = active.shape[0]
    rank_width = adapter_in.shape[2]
    local_adapters = adapter_in.shape[0]
    owned_ids = dp_index * local_adapters + jnp.arange(local_adapters, dtype=jnp.int32)
    selector = (active[:, None] == owned_ids[None, :]).astype(jnp.bfloat16)
    out_cols = lax.dynamic_slice_in_dim(adapter_out, col_start, col_width, axis=2)
    picked_in = jnp.einsum(
        "ji,isr->jsr", selector, adapter_in, preferred_element_type=jnp.float32
    ).astype(jnp.bfloat16)
    picked_out = jnp.einsum(
        "ji,ird->jrd", selector, out_cols, preferred_element_type=jnp.float32
    ).astype(jnp.bfloat16)
    picked_in, picked_out = lax.psum((picked_in, picked_out), "dp")
    gathered = lax.all_gather(hidden, "mp", axis=1, tiled=True)
    values = gathered.astype(jnp.float32)
    factor = lax.rsqrt(jnp.mean(values * values, axis=-1, keepdims=True) + 1e-06)
    normed = (values * factor * norm_gain.astype(jnp.float32)).astype(jnp.bfloat16)
    width = normed.shape[1]
    shared_lin = jnp.dot(normed, shared_gate, preferred_element_type=jnp.float32)
    shared_pre = jnp.dot(normed, shared_up, preferred_element_type=jnp.float32)
    shared_act = (jax.nn.silu(shared_lin) * shared_pre).astype(jnp.bfloat16)
    request_end = jnp.cumsum(lengths)
    positions = dp_index * tok_rows + jnp.arange(tok_rows, dtype=jnp.int32)
    request_of = jnp.sum((request_end[None, :] <= positions[:, None]).astype(jnp.int32), axis=1)
    request_hot = (
        request_of[:, None] == jnp.arange(lengths.shape[0], dtype=jnp.int32)[None, :]
    ).astype(jnp.int32)
    slot_of = jnp.sum(request_hot * request_adapter[None, :], axis=1)
    chosen = (slot_of[:, None] == jnp.arange(active_count, dtype=jnp.int32)[None, :]).astype(
        jnp.float32
    )
    in_matrix = jnp.transpose(picked_in, (1, 0, 2)).reshape(
        shared_act.shape[1], active_count * rank_width
    )
    lowrank = jnp.dot(shared_act, in_matrix, preferred_element_type=jnp.float32)
    lowrank_sel = jnp.sum(
        lowrank.reshape(tok_rows, active_count, rank_width) * chosen[:, :, None], axis=1
    )
    lowrank_sel = lax.psum(lowrank_sel, "mp")
    lowrank = (chosen[:, :, None] * lowrank_sel[:, None, :]).reshape(
        tok_rows, active_count * rank_width
    )
    adapted = jnp.dot(
        lowrank,
        picked_out.reshape(active_count * rank_width, col_width).astype(jnp.float32),
        precision=lax.Precision.HIGHEST,
    )
    flat_routes = routes.reshape(-1)
    expert_hot = (
        flat_routes[:, None] == jnp.arange(total_experts, dtype=jnp.int32)[None, :]
    ).astype(jnp.int32)
    earlier = jnp.cumsum(expert_hot, axis=0) - expert_hot
    position = jnp.sum(earlier * expert_hot, axis=1)
    slot_index = (flat_routes * capacity + position).reshape(tok_rows, top_count)
    slot_count = total_experts * capacity
    slot_hit = slot_index[:, :, None] == jnp.arange(slot_count, dtype=jnp.int32)[None, None, :]
    dispatch = jnp.any(slot_hit, axis=1).astype(jnp.bfloat16)
    send_rows = jnp.einsum(
        "ts,td->sd", dispatch, normed, preferred_element_type=jnp.float32
    ).astype(jnp.bfloat16)
    send_rows = send_rows.reshape(dp_count, local_experts, capacity, width)
    returned = lax.all_to_all(
        experts_apply(
            lax.all_to_all(send_rows, "dp", split_axis=0, concat_axis=0, tiled=True),
            expert_gate,
            expert_up,
            expert_down,
        ).astype(jnp.bfloat16),
        "dp",
        split_axis=0,
        concat_axis=0,
        tiled=True,
    )
    returned = returned.reshape(slot_count, width)
    combine = jnp.sum(jnp.where(slot_hit, route_weights[:, :, None], 0.0), axis=1)
    combine_hi = combine.astype(jnp.bfloat16)
    combine_lo = (combine - combine_hi.astype(jnp.float32)).astype(jnp.bfloat16)
    routed = jnp.dot(combine_hi, returned, preferred_element_type=jnp.float32) + jnp.dot(
        combine_lo, returned, preferred_element_type=jnp.float32
    )
    partial_out = jnp.dot(shared_act, shared_down, preferred_element_type=jnp.float32) + routed
    own_cols = lax.dynamic_slice_in_dim(partial_out, col_start, col_width, axis=1) + adapted
    partial_out = lax.dynamic_update_slice_in_dim(partial_out, own_cols, col_start, axis=1)
    return lax.psum_scatter(partial_out.astype(jnp.bfloat16), "mp", scatter_dimension=1, tiled=True)


def solution(mesh):
    in_specs = (
        P("dp", "mp"),
        P(),
        P(None, "mp"),
        P(None, "mp"),
        P("mp", None),
        P("dp", None, "mp"),
        P("dp", None, "mp"),
        P("dp", "mp", None),
        P("dp", "mp", None),
        P("dp", None, None),
        P(),
        P(),
        P(),
        P("dp", None),
        P("dp", None),
    )
    out_specs = P("dp", "mp")
    return jax.shard_map(body, mesh=mesh, in_specs=in_specs, out_specs=out_specs, check_vma=False)
```

profile of v0, /device:TPU:0, one launch (start us, length us, event | category | flops | bytes accessed | tf_op | source)
XLA Modules:
  0.0 315.9 jit_solution(4285871344129331172)
XLA Ops:
  6.5 0.8 copy.60
  7.7 1.8 reduce-window.18
  10.1 0.7 multiply_add_fusion
  11.3 14.9 %all_gather.3 = bf16[128,2560]{1,0:T(8,128)(2,1)S(1)} all-gather(bf16[128,640]{1,0:T(8,128)(2,1)} %param.15), channel_id=1, replica_groups=mesh['dp'=32,'mp'=4] {'mp'}, dimensions={1}, use_global_device_ids=true | all-gather | bytes 819200 | tf_op jit(solution)/shard_map/all_gather | solution.py:57
  27.2 1.6 convolution_convert_fusion.1
  28.8 69.5 %all_to_all.10 = bf16[32,2,16,2560]{3,2,1,0:T(8,128)(2,1)S(1)} all-to-all(bf16[32,2,16,2560]{3,2,1,0:T(8,128)(2,1)S(1)} %bitcast.98), channel_id=1, replica_groups=mesh['dp'=32,'mp'=4] {'dp'}, dimensions={0} | all-to-all | bytes 10485760 | tf_op jit(solution)/shard_map/all_to_all | solution.py:107
  98.3 2.3 copy-done.1
  100.6 2.9 fusion.3
  103.5 12.8 %fusion = bf16[32,2,16,2560]{3,2,0,1:T(8,128)(2,1)} fusion(bf16[2,384,2560]{2,1,0:T(8,128)(2,1)} %param.22, f32[2,32,16,384]{3,2,1,0:T(8,128)S(1)} %fusion.3, bf16[2,2560,384]{2,1,0:T(8,128)(2,1)} %param.21, bf16[32,2,16,2560]{3,2,1,0:T(8,128)(2,1)} %copy-done.1), kind=kOutput, calls=%fused_computation.2 | convolution fusion | flops 4031512576 | bytes 19922944 | tf_op jit(solution)/shard_map/sjcf,jfd->sjcd/dot_general | solution.py:13
  116.3 5.3 %copy.66 = bf16[32,2,16,2560]{3,2,1,0:T(8,128)(2,1)} copy(bf16[32,2,16,2560]{3,2,0,1:T(8,128)(2,1)} %fusion) | data formatting | bytes 10485760 | tf_op jit(solution)/shard_map/convert_element_type | solution.py:111
  121.5 5.0 %all-to-all-start.1 = ((bf16[32,2,16,2560]{3,2,1,0:T(8,128)(2,1)}), bf16[32,2,16,2560]{3,2,1,0:T(8,128)(2,1)}, u32[]{:S(2)}, u32[]{:S(2)}) async-start(bf16[32,2,16,2560]{3,2,1,0:T(8,128)(2,1)} %copy.66), calls=%async_computation.1 | async-start | bytes 10485760 | tf_op jit(solution)/shard_map/all_to_all | solution.py:105
  127.1 0.9 copy.95
  128.0 1.1 convolution_convert_fusion.3
  130.3 3.2 fusion.57
  133.5 0.8 fusion.26
  134.3 1.3 copy-done.2
  136.3 131.0 %all-reduce.3.cloned.1.call-done = (bf16[16,16,640]{2,0,1:T(8,128)(2,1)}, bf16[16,16,768]{2,1,0:T(8,128)(2,1)}) async-done(((bf16[16,16,640]{2,0,1:T(8,128)(2,1)}, bf16[16,16,768]{2,1,0:T(8,128)(2,1)}), (bf16[16,16,640]{2,0,1:T(8,128)(2,1)}, bf16[16,16,768]{2,1,0:T(8,128)(2,1)})) %all-reduce.3.cloned.1.call-update) | async-done | bytes 720912 | tf_op jit(solution)/shard_map/psum | solution.py:56
  267.3 1.3 fusion.29
  268.6 10.8 %psum.22 = f32[128,16]{0,1:T(8,128)S(1)} all-reduce(f32[128,16]{0,1:T(8,128)S(1)} %fusion.29), channel_id=1, replica_groups=mesh['dp'=32,'mp'=4] {'mp'}, use_global_device_ids=true, to_apply=%region_11.12 | all-reduce | flops 2048 | bytes 16384 | tf_op jit(solution)/shard_map/psum | solution.py:82
  279.4 3.3 %fusion.39 = f32[128,2560]{1,0:T(8,128)S(1)} fusion(bf16[1024,2560]{1,0:T(8,128)(2,1)} %bitcast.11, f32[128,1024]{1,0:T(8,128)S(1)} %select_reduce_fusion), kind=kOutput, calls=%fused_computation.53 | convolution fusion | flops 671219712 | bytes 7077888 | tf_op jit(solution)/shard_map/dot_general | solution.py:121
  282.7 3.5 %fusion.8 = f32[128,2560]{1,0:T(8,128)S(1)} fusion(f32[128,2560]{1,0:T(8,128)S(1)} %fusion.59, f32[128,2560]{1,0:T(8,128)S(1)} %fusion.39, bf16[1024,2560]{1,0:T(8,128)(2,1)} %bitcast.11, f32[128,1024]{1,0:T(8,128)S(1)} %select_reduce_fusion), kind=kOutput, calls=%fused_computation.11 | convolution fusion | flops 672268288 | bytes 9699328 | tf_op jit(solution)/shard_map/dot_general | solution.py:121
  286.7 1.1 copy.75
  287.8 19.6 %reduce-scatter.4.cloned.1.call-done = bf16[640,128]{1,0:T(8,128)(2,1)} async-done(((bf16[2560,128]{1,0:T(8,128)(2,1)}), bf16[640,128]{1,0:T(8,128)(2,1)}) %reduce-scatter.4.cloned.1.call-update) | async-done | bytes 163856
  307.4 1.7 copy.76
  (51 shorter events, 5.1 us)
Async XLA Ops:
  6.5 121.4 %copy-start = (bf16[2,16,2560]{2,1,0:T(8,128)(2,1)S(1)}, bf16[2,16,2560]{2,1,0:T(8,128)(2,1)}, u32[]{:S(2)}) copy-start(bf16[2,16,2560]{2,1,0:T(8,128)(2,1)} %param.24) | copy-start | bytes 491524
  28.8 71.8 %copy-start.8 = (bf16[2,2560,384]{2,1,0:T(8,128)(2,1)S(1)}, bf16[2,2560,384]{2,1,0:T(8,128)(2,1)}, u32[]{:S(2)}) copy-start(bf16[2,2560,384]{2,1,0:T(8,128)(2,1)} %param.20) | copy-start | bytes 11796484
  98.3 2.3 copy-start.1
  121.5 5.1 %copy-start.4 = (bf16[2,768,16]{1,2,0:T(8,128)(2,1)S(1)}, bf16[2,768,16]{1,2,0:T(8,128)(2,1)}, u32[]{:S(2)}) copy-start(bf16[2,768,16]{1,2,0:T(8,128)(2,1)} %param.23) | copy-start | bytes 147460
  121.5 5.1 %copy-start.6 = (s32[16]{0:T(128)S(1)}, s32[16]{0:T(128)}, u32[]{:S(2)}) copy-start(s32[16]{0:T(128)} %param.25) | copy-start | bytes 196
  121.5 7.8 %copy-start.7 = (s32[64]{0:T(128)S(1)}, s32[64]{0:T(128)}, u32[]{:S(2)}) copy-start(s32[64]{0:T(128)} %param.26) | copy-start | bytes 772
  121.5 8.2 %copy-start.10 = (s32[64]{0:T(128)S(1)}, s32[64]{0:T(128)}, u32[]{:S(2)}) copy-start(s32[64]{0:T(128)} %param.27) | copy-start | bytes 772
  121.5 8.3 %copy-start.5 = (f32[128,6]{0,1:T(8,128)S(1)}, f32[128,6]{0,1:T(8,128)}, u32[]{:S(2)}) copy-start(f32[128,6]{0,1:T(8,128)} %param.29) | copy-start | bytes 9220
  121.5 157.8 %all-to-all-start.1 = ((bf16[32,2,16,2560]{3,2,1,0:T(8,128)(2,1)}), bf16[32,2,16,2560]{3,2,1,0:T(8,128)(2,1)}, u32[]{:S(2)}, u32[]{:S(2)}) async-start(bf16[32,2,16,2560]{3,2,1,0:T(8,128)(2,1)} %copy.66), calls=%async_computation.1 | async-start | bytes 10485760 | tf_op jit(solution)/shard_map/all_to_all | solution.py:105
  126.6 140.7 %all-reduce.3.cloned.1.call-start = ((), (), s32[]{:S(2)}) async-start(), calls=%async_computation.4 | async-start | bytes 1441792 | tf_op jit(solution)/shard_map/psum | solution.py:56
  129.1 178.2 %reduce-scatter.4.cloned.1.call-start = ((), (), s32[]{:S(2)}) async-start(), calls=%async_computation.3 | async-start | bytes 819200
  129.7 3.8 %copy-start.9 = (bf16[2560,768]{1,0:T(8,128)(2,1)S(1)}, bf16[2560,768]{1,0:T(8,128)(2,1)}, u32[]{:S(2)}) copy-start(bf16[2560,768]{1,0:T(8,128)(2,1)} %param.18) | copy-start | bytes 11796484
  133.5 2.1 copy-start.2
  282.7 3.5 %copy-start.3 = (bf16[16,16,640]{2,0,1:T(8,128)(2,1)S(1)}, bf16[16,16,640]{2,0,1:T(8,128)(2,1)}, u32[]{:S(2)}) copy-start(bf16[16,16,640]{2,0,1:T(8,128)(2,1)} %get-tuple-element.5) | copy-start | bytes 983044
Sparse Core Ops, SparseCore 0:
  130.8 136.4 all-reduce.2
  287.9 19.4 reduce-scatter.3
where the time goes:
time: 316 us
  waiting for transfers between devices  151 us (48%)
  blocking collectives  95.2 us (30%)
  matrix products  31.9 us (10%)
  local copies, waits for them, and re-layouts  14.3 us (5%)
  between operations  13.7 us (4%)
  starting transfers between devices  5.27 us (2%)
  other arithmetic  4.99 us (2%)
    psum x1, waiting for transfers between devices, body(): picked_in, picked_out = lax.psum((picked_in, picked_out), 'dp')  131 us
    all_to_all x1, blocking collectives, body(): lax.all_to_all(send_rows, 'dp', split_axis=0, concat_axis=0, tiled=True)  69.5 us
    unnamed x3, waiting for transfers between devices  19.6 us
    all_gather x1, blocking collectives, body(): gathered = lax.all_gather(hidden, 'mp', axis=1, tiled=True)  14.9 us
    dot_general x1, matrix products, experts_apply(): jnp.einsum('sjcf,jfd->sjcd', inner, expert_down, preferred_element_type=j...  12.8 us
    psum x1, blocking collectives, body(): lowrank_sel = lax.psum(lowrank_sel, 'mp')  10.8 us
    unnamed x25, local copies, waits for them, and re-layouts  7.3 us
  transfers between devices with their start and end apart: 3, of which 2 were waited for; matrix products, arithmetic and copies ran while one was open for 3% of the time, Pallas kernels for 0%

commit v1 on v0

--- a/solution.py
+++ b/solution.py
@@ -54,7 +54,9 @@
         "ji,ird->jrd", selector, out_cols, preferred_element_type=jnp.float32
     ).astype(jnp.bfloat16)
     picked_in, picked_out = lax.psum((picked_in, picked_out), "dp")
-    gathered = lax.all_gather(hidden, "mp", axis=1, tiled=True)
+    gathered = jnp.concatenate(
+        lax.all_to_all(jnp.stack([hidden] * lax.axis_size("mp")), "mp", 0, 0), axis=1
+    )
     values = gathered.astype(jnp.float32)
     factor = lax.rsqrt(jnp.mean(values * values, axis=-1, keepdims=True) + 1e-06)
     normed = (values * factor * norm_gain.astype(jnp.float32)).astype(jnp.bfloat16)

time: 316 us -> 316 us (level)
  blocking collectives: 95.2 us -> 80.3 us
  waiting for transfers between devices: 151 us -> 157 us
  starting transfers between devices: 5.27 us -> 10.7 us
    all_gather x1 -> x0, blocking collectives: 14.9 us -> none  [body(): gathered = lax.all_gather(hidden, 'mp', axis=1, tiled=True)]
    all_to_all x0 -> x1, waiting for transfers between devices: none -> 5.44 us  [body(): lax.all_to_all(jnp.stack([hidden] * lax.axis_size('mp')), 'mp', 0, 0)]
    all_to_all x0 -> x1, starting transfers between devices: none -> 5.42 us  [body(): lax.all_to_all(jnp.stack([hidden] * lax.axis_size('mp')), 'mp', 0, 0)]
    unnamed x25 -> x24, local copies, waits for them, and re-layouts: 7.3 us -> 7.05 us
  transfers between devices with their start and end apart: 3 -> 4, of which waited for: 2 -> 3; matrix products, arithmetic and copies ran while one was open for 3% -> 5% of each run, Pallas kernels for 0% -> 0%
where the time goes in v1:
time: 316 us
  waiting for transfers between devices  157 us (50%)
  blocking collectives  80.3 us (25%)
  matrix products  33.9 us (11%)
  local copies, waits for them, and re-layouts  14.9 us (5%)
  between operations  13.7 us (4%)
  starting transfers between devices  10.7 us (3%)
  other arithmetic  5.53 us (2%)
    psum x1, waiting for transfers between devices, body(): picked_in, picked_out = lax.psum((picked_in, picked_out), 'dp')  132 us
    all_to_all x1, blocking collectives, body(): lax.all_to_all(send_rows, 'dp', split_axis=0, concat_axis=0, tiled=True)  69.5 us
    unnamed x3, waiting for transfers between devices  19.6 us
    dot_general x1, matrix products, experts_apply(): jnp.einsum('sjcf,jfd->sjcd', inner, expert_down, preferred_element_type=j...  12.8 us
    psum x1, blocking collectives, body(): lowrank_sel = lax.psum(lowrank_sel, 'mp')  10.8 us
    unnamed x24, local copies, waits for them, and re-layouts  7.05 us
  transfers between devices with their start and end apart: 4, of which 3 were waited for; matrix products, arithmetic and copies ran while one was open for 5% of the time, Pallas kernels for 0%

profile of v1, /device:TPU:0, one launch (start us, length us, event | category | flops | bytes accessed | tf_op | source)
XLA Modules:
  0.0 315.8 jit_solution(2823657065508086172)
XLA Ops:
  6.5 1.1 copy.63
  7.6 0.9 stack.2
  8.6 5.4 %all-to-all-start = ((bf16[4,128,640]{1,2,0:T(8,128)(2,1)}), bf16[4,128,640]{1,2,0:T(8,128)(2,1)S(1)}, u32[]{:S(2)}, u32[]{:S(2)}) async-start(bf16[4,128,640]{1,2,0:T(8,128)(2,1)} %stack.2), calls=%async_computation | async-start | bytes 1310720 | tf_op jit(solution)/shard_map/all_to_all | solution.py:58
  15.1 1.8 reduce-window.18
  19.4 5.4 %all-to-all-done = bf16[4,128,640]{1,2,0:T(8,128)(2,1)S(1)} async-done(((bf16[4,128,640]{1,2,0:T(8,128)(2,1)}), bf16[4,128,640]{1,2,0:T(8,128)(2,1)S(1)}, u32[]{:S(2)}, u32[]{:S(2)}) %all-to-all-start) | async-done | bytes 655392 | tf_op jit(solution)/shard_map/all_to_all | solution.py:58
  25.7 1.6 convolution_convert_fusion
  27.2 69.5 %all_to_all.15 = bf16[32,2,16,2560]{3,2,1,0:T(8,128)(2,1)S(1)} all-to-all(bf16[32,2,16,2560]{3,2,1,0:T(8,128)(2,1)S(1)} %bitcast.108), channel_id=1, replica_groups=mesh['dp'=32,'mp'=4] {'dp'}, dimensions={0} | all-to-all | bytes 10485760 | tf_op jit(solution)/shard_map/all_to_all | solution.py:109
  96.8 2.3 copy-done.1
  99.1 2.9 fusion.3
  101.9 12.8 %fusion = bf16[32,2,16,2560]{3,2,0,1:T(8,128)(2,1)} fusion(bf16[2,384,2560]{2,1,0:T(8,128)(2,1)} %param.22, f32[2,32,16,384]{3,2,1,0:T(8,128)S(1)} %fusion.3, bf16[2,2560,384]{2,1,0:T(8,128)(2,1)} %param.21, bf16[32,2,16,2560]{3,2,1,0:T(8,128)(2,1)} %copy-done.1), kind=kOutput, calls=%fused_computation.2 | convolution fusion | flops 4031512576 | bytes 19922944 | tf_op jit(solution)/shard_map/sjcf,jfd->sjcd/dot_general | solution.py:13
  114.7 5.3 %copy.70 = bf16[32,2,16,2560]{3,2,1,0:T(8,128)(2,1)} copy(bf16[32,2,16,2560]{3,2,0,1:T(8,128)(2,1)} %fusion) | data formatting | bytes 10485760 | tf_op jit(solution)/shard_map/convert_element_type | solution.py:113
  120.0 5.0 %all-to-all-start.2 = ((bf16[32,2,16,2560]{3,2,1,0:T(8,128)(2,1)}), bf16[32,2,16,2560]{3,2,1,0:T(8,128)(2,1)}, u32[]{:S(2)}, u32[]{:S(2)}) async-start(bf16[32,2,16,2560]{3,2,1,0:T(8,128)(2,1)} %copy.70), calls=%async_computation.2 | async-start | bytes 10485760 | tf_op jit(solution)/shard_map/all_to_all | solution.py:107
  125.5 0.9 copy.99
  126.4 1.1 convolution_convert_fusion.3
  128.8 3.2 %fusion.55 = f32[128,768]{1,0:T(8,128)S(1)} fusion(bf16[128,2560]{0,1:T(8,128)(2,1)S(1)} %fusion.23, bf16[2560,768]{1,0:T(8,128)(2,1)} %param.17), kind=kOutput, calls=%fused_computation.78 | convolution fusion | flops 503316480 | bytes 4980736 | tf_op jit(solution)/shard_map/dot_general | solution.py:64
  132.7 131.7 %all-reduce.3.cloned.1.call-done = (bf16[16,16,640]{2,0,1:T(8,128)(2,1)}, bf16[16,16,768]{2,1,0:T(8,128)(2,1)}) async-done(((bf16[16,16,640]{2,0,1:T(8,128)(2,1)}, bf16[16,16,768]{2,1,0:T(8,128)(2,1)}), (bf16[16,16,640]{2,0,1:T(8,128)(2,1)}, bf16[16,16,768]{2,1,0:T(8,128)(2,1)})) %all-reduce.3.cloned.1.call-update) | async-done | bytes 720912 | tf_op jit(solution)/shard_map/psum | solution.py:56
  264.4 1.3 fusion.28
  265.6 10.8 %psum.22 = f32[128,16]{0,1:T(8,128)S(1)} all-reduce(f32[128,16]{0,1:T(8,128)S(1)} %fusion.28), channel_id=1, replica_groups=mesh['dp'=32,'mp'=4] {'mp'}, use_global_device_ids=true, to_apply=%region_11.12 | all-reduce | flops 2048 | bytes 16384 | tf_op jit(solution)/shard_map/psum | solution.py:84
  276.4 2.8 fusion.56
  279.2 3.3 %fusion.39 = f32[128,2560]{1,0:T(8,128)S(1)} fusion(bf16[1024,2560]{1,0:T(8,128)(2,1)} %bitcast.13, f32[128,1024]{1,0:T(8,128)S(1)} %select_reduce_fusion), kind=kOutput, calls=%fused_computation.53 | convolution fusion | flops 671219712 | bytes 7077888 | tf_op jit(solution)/shard_map/dot_general | solution.py:123
  282.6 3.5 %fusion.8 = f32[128,2560]{1,0:T(8,128)S(1)} fusion(f32[128,2560]{1,0:T(8,128)S(1)} %fusion.56, f32[128,2560]{1,0:T(8,128)S(1)} %fusion.39, bf16[1024,2560]{1,0:T(8,128)(2,1)} %bitcast.13, f32[128,1024]{1,0:T(8,128)S(1)} %select_reduce_fusion), kind=kOutput, calls=%fused_computation.11 | convolution fusion | flops 672268288 | bytes 9699328 | tf_op jit(solution)/shard_map/dot_general | solution.py:123
  286.5 1.1 copy.79
  287.6 19.6 %reduce-scatter.4.cloned.1.call-done = bf16[640,128]{1,0:T(8,128)(2,1)} async-done(((bf16[2560,128]{1,0:T(8,128)(2,1)}), bf16[640,128]{1,0:T(8,128)(2,1)}) %reduce-scatter.4.cloned.1.call-update) | async-done | bytes 163856
  307.2 1.7 copy.80
  (53 shorter events, 7.2 us)
Async XLA Ops:
  6.5 119.9 %copy-start = (bf16[2,16,2560]{2,1,0:T(8,128)(2,1)S(1)}, bf16[2,16,2560]{2,1,0:T(8,128)(2,1)}, u32[]{:S(2)}) copy-start(bf16[2,16,2560]{2,1,0:T(8,128)(2,1)} %param.24) | copy-start | bytes 491524
  8.6 16.3 %all-to-all-start = ((bf16[4,128,640]{1,2,0:T(8,128)(2,1)}), bf16[4,128,640]{1,2,0:T(8,128)(2,1)S(1)}, u32[]{:S(2)}, u32[]{:S(2)}) async-start(bf16[4,128,640]{1,2,0:T(8,128)(2,1)} %stack.2), calls=%async_computation | async-start | bytes 1310720 | tf_op jit(solution)/shard_map/all_to_all | solution.py:58
  27.2 71.9 %copy-start.8 = (bf16[2,2560,384]{2,1,0:T(8,128)(2,1)S(1)}, bf16[2,2560,384]{2,1,0:T(8,128)(2,1)}, u32[]{:S(2)}) copy-start(bf16[2,2560,384]{2,1,0:T(8,128)(2,1)} %param.20) | copy-start | bytes 11796484
  96.8 2.3 copy-start.1
  120.0 5.1 %copy-start.4 = (bf16[2,768,16]{1,2,0:T(8,128)(2,1)S(1)}, bf16[2,768,16]{1,2,0:T(8,128)(2,1)}, u32[]{:S(2)}) copy-start(bf16[2,768,16]{1,2,0:T(8,128)(2,1)} %param.23) | copy-start | bytes 147460
  120.0 5.1 %copy-start.6 = (s32[16]{0:T(128)S(1)}, s32[16]{0:T(128)}, u32[]{:S(2)}) copy-start(s32[16]{0:T(128)} %param.25) | copy-start | bytes 196
  120.0 7.8 %copy-start.7 = (s32[64]{0:T(128)S(1)}, s32[64]{0:T(128)}, u32[]{:S(2)}) copy-start(s32[64]{0:T(128)} %param.26) | copy-start | bytes 772
  120.0 8.3 %copy-start.9 = (s32[64]{0:T(128)S(1)}, s32[64]{0:T(128)}, u32[]{:S(2)}) copy-start(s32[64]{0:T(128)} %param.27) | copy-start | bytes 772
  120.0 8.3 %copy-start.5 = (f32[128,6]{0,1:T(8,128)S(1)}, f32[128,6]{0,1:T(8,128)}, u32[]{:S(2)}) copy-start(f32[128,6]{0,1:T(8,128)} %param.29) | copy-start | bytes 9220
  120.0 159.2 %all-to-all-start.2 = ((bf16[32,2,16,2560]{3,2,1,0:T(8,128)(2,1)}), bf16[32,2,16,2560]{3,2,1,0:T(8,128)(2,1)}, u32[]{:S(2)}, u32[]{:S(2)}) async-start(bf16[32,2,16,2560]{3,2,1,0:T(8,128)(2,1)} %copy.70), calls=%async_computation.2 | async-start | bytes 10485760 | tf_op jit(solution)/shard_map/all_to_all | solution.py:107
  125.0 139.3 %all-reduce.3.cloned.1.call-start = ((), (), s32[]{:S(2)}) async-start(), calls=%async_computation.5 | async-start | bytes 1441792 | tf_op jit(solution)/shard_map/psum | solution.py:56
  127.6 179.7 %reduce-scatter.4.cloned.1.call-start = ((), (), s32[]{:S(2)}) async-start(), calls=%async_computation.4 | async-start | bytes 819200
  128.1 3.8 %copy-start.2 = (bf16[2560,768]{1,0:T(8,128)(2,1)S(1)}, bf16[2560,768]{1,0:T(8,128)(2,1)}, u32[]{:S(2)}) copy-start(bf16[2560,768]{1,0:T(8,128)(2,1)} %param.18) | copy-start | bytes 11796484
  282.6 3.5 %copy-start.3 = (bf16[16,16,640]{2,0,1:T(8,128)(2,1)S(1)}, bf16[16,16,640]{2,0,1:T(8,128)(2,1)}, u32[]{:S(2)}) copy-start(bf16[16,16,640]{2,0,1:T(8,128)(2,1)} %get-tuple-element.5) | copy-start | bytes 983044
Sparse Core Ops, SparseCore 0:
  129.2 135.0 all-reduce.2
  287.8 19.4 reduce-scatter.3
